TPU v7x, 32 devices: a whole 2x2x4 slice. The times are simulated.
32 devices in a mesh: track: 4 (over z), cross: 8 (over y, x, core).
Axes of the slice: x: 2, y: 2, z: 4, core: 2. Of those that a mesh axis runs over, the one named last changes fastest.
Arguments:
- cube: bfloat16 [1024, 256, 224], P('track', 'cross'), may hold values from -60 to 113, as said below
Outputs:
- scores: float32 [1024, 256], P('track', 'cross')
Inputs may be any that keep to these rules, and one draw needn't show every extreme that they name: `cube`: A positive radiance level per band plus noise, scaled per band and by position.
All inputs are finite; a program needn't handle non-finite values.
Results may differ from a plain program's by a relative error of at most 0.0003.
Values may be sent and summed in bfloat16 or wider, within the bound.
No kernel may reach another device: no remote copies, remote signals or barrier semaphores. Data moves between devices by JAX's collectives and lax.ppermute only.
A program may use at most 64 MiB of HBM per device.

v0:
```python
import jax
import jax.numpy as jnp
from jax import lax
from jax.sharding import PartitionSpec as P

HALF = 15
LOAD = 0.02


def with_halo(block, sides, width):
    for axis, dim in sides:
        count = lax.axis_size(axis)
        forward = [(i, i + 1) for i in range(count - 1)]
        backward = [(target, source) for source, target in forward]
        low = lax.ppermute(
            lax.slice_in_dim(block, block.shape[dim] - width, None, axis=dim), axis, forward
        )
        high = lax.ppermute(lax.slice_in_dim(block, 0, width, axis=dim), axis, backward)
        block = jnp.concatenate([low, block, high], axis=dim)
    return block


def band_matrix(rows_in, rows_out, dtype):
    source = jnp.arange(rows_in)[:, None]
    target = jnp.arange(rows_out)[None, :]
    inside = (source >= target) & (source <= target + 2 * HALF)
    return inside.astype(dtype)


def window_count(first, local, total):
    index = first + jnp.arange(local)
    upper = jnp.minimum(index + HALF, total - 1)
    lower = jnp.maximum(index - HALF, 0)
    return (upper - lower + 1).astype(jnp.float32)


def sum_pixels(values, width, dtype):
    weights = band_matrix(width + 2 * HALF, width, dtype)
    return jnp.einsum(
        "lqb,qp->lpb", values, weights, precision=None, preferred_element_type=jnp.float32
    )


def sum_lines(values, height, dtype, precision):
    weights = band_matrix(height + 2 * HALF, height, dtype)
    return jnp.einsum(
        "kpb,kl->lpb", values, weights, precision=precision, preferred_element_type=jnp.float32
    )


def shards(cube):
    lines_dev, pix_dev, bands = cube.shape
    n_track = lax.axis_size("track")
    n_cross = lax.axis_size("cross")
    total_lines = lines_dev * n_track
    total_pix = pix_dev * n_cross
    highest = lax.Precision.HIGHEST
    extended = with_halo(cube, (("track", 0), ("cross", 1)), HALF)
    across = sum_pixels(extended, pix_dev, jnp.bfloat16)
    window = sum_lines(across, lines_dev, jnp.float32, highest)
    line_count = window_count(lax.axis_index("track") * lines_dev, lines_dev, total_lines)
    pixel_count = window_count(lax.axis_index("cross") * pix_dev, pix_dev, total_pix)
    count = line_count[:, None, None] * pixel_count[None, :, None]
    residual = cube.astype(jnp.float32) - window / count
    flat = residual.reshape(lines_dev * pix_dev, bands)
    flat_bf = flat.astype(jnp.bfloat16)
    partial_cov = jnp.dot(flat_bf.T, flat_bf, preferred_element_type=jnp.float32)
    covariance = lax.psum(partial_cov, ("track", "cross")) / (total_lines * total_pix)
    identity = jnp.eye(bands, dtype=jnp.float32)
    loaded = covariance + LOAD * (jnp.trace(covariance) / bands) * identity
    factor = jnp.linalg.cholesky(loaded)
    inverse = jax.scipy.linalg.solve_triangular(factor, identity, lower=True)
    whitened = jnp.dot(flat, inverse.T, precision=highest, preferred_element_type=jnp.float32)
    scores = jnp.sum(whitened * whitened, axis=1) / bands
    return scores.reshape(lines_dev, pix_dev)


def solution(mesh):
    return jax.shard_map(
        shards,
        mesh=mesh,
        in_specs=(P("track", "cross", None),),
        out_specs=P("track", "cross"),
        check_vma=False,
    )
```

profile of v0, /device:TPU:1, one launch (start us, length us, event | category | flops | bytes accessed | tf_op | source)
XLA Modules:
  0.0 329.4 jit_solution(2984762335970636967)
XLA Ops:
  6.5 0.0 all-reduce.5.cloned.1.call-start
  6.5 7.8 %copy.6 = bf16[256,32,224]{2,1,0:T(8,128)(2,1)} copy(bf16[256,32,224]{0,2,1:T(8,128)(2,1)} %param.1) | data formatting | bytes 7340032 | tf_op args[0]
  14.4 1.1 fusion.46
  15.5 4.0 %collective-permute-start = (bf16[15,32,224]{2,1,0:T(8,128)(2,1)S(1)}, bf16[15,32,224]{2,1,0:T(8,128)(2,1)S(1)}, u32[]{:S(2)}, u32[]{:S(2)}) collective-permute-start(bf16[15,32,224]{2,1,0:T(8,128)(2,1)S(1)} %get-tuple-element.27), channel_id=1, source_target_pairs={{0,8},{8,16},{16,24},{1,9},{9,17},{17,25},{2,10},{10,18},{18,26},{... | collective-permute-start | bytes 645128 | tf_op jit(solution)/shard_map/ppermute | solution.py:15
  19.5 1.3 collective-permute-start.1
  20.8 3.3 collective-permute-done
  24.1 3.8 %collective-permute-done.1 = bf16[15,32,224]{2,1,0:T(8,128)(2,1)S(1)} collective-permute-done((bf16[15,32,224]{2,1,0:T(8,128)(2,1)S(1)}, bf16[15,32,224]{2,1,0:T(8,128)(2,1)S(1)}, u32[]{:S(2)}, u32[]{:S(2)}) %collective-permute-start.1) | collective-permute-done | bytes 215072 | tf_op jit(solution)/shard_map/ppermute | solution.py:18
  27.9 2.7 pad_maximum_fusion
  30.7 1.0 fusion.45
  31.7 0.8 copy.9
  32.5 4.9 %collective-permute-start.2 = (bf16[286,15,224]{2,0,1:T(8,128)(2,1)S(1)}, bf16[286,15,224]{2,0,1:T(8,128)(2,1)}, u32[]{:S(2)}, u32[]{:S(2)}) collective-permute-start(bf16[286,15,224]{2,0,1:T(8,128)(2,1)S(1)} %copy.9), channel_id=1, source_target_pairs={{0,1},{1,2},{2,3},{3,4},{4,5},{5,6},{6,7},{8,9},{9,10},{10,11},{11... | collective-permute-start | bytes 5765768 | tf_op jit(solution)/shard_map/ppermute | solution.py:15
  37.4 2.1 copy.10
  39.6 1.9 collective-permute-start.3
  41.5 0.0 copy-start.1
  41.6 0.1 broadcast_multiply_fusion.1
  41.6 20.0 %collective-permute-done.2 = bf16[286,15,224]{2,0,1:T(8,128)(2,1)} collective-permute-done((bf16[286,15,224]{2,0,1:T(8,128)(2,1)S(1)}, bf16[286,15,224]{2,0,1:T(8,128)(2,1)}, u32[]{:S(2)}, u32[]{:S(2)}) %collective-permute-start.2) | collective-permute-done | bytes 1921952 | tf_op jit(solution)/shard_map/ppermute | solution.py:15
  61.6 2.9 copy.11
  64.5 22.6 %collective-permute-done.3 = bf16[286,15,224]{2,0,1:T(8,128)(2,1)} collective-permute-done((bf16[286,15,224]{2,0,1:T(8,128)(2,1)}, bf16[286,15,224]{2,0,1:T(8,128)(2,1)}, u32[]{:S(2)}, u32[]{:S(2)}) %collective-permute-start.3) | collective-permute-done | bytes 1921952 | tf_op jit(solution)/shard_map/ppermute | solution.py:18
  87.1 2.9 copy.12
  89.9 0.0 copy-done.1
  89.9 0.0 copy-start.2
  89.9 15.9 %fusion.14 = f32[286,32,224]{2,1,0:T(8,128)} fusion(bf16[286,15,224]{2,1,0:T(8,128)(2,1)S(1)} %copy.12, bf16[15,32,224]{2,1,0:T(8,128)(2,1)S(1)} %collective-permute-done.1, bf16[256,32,224]{2,1,0:T(8,128)(2,1)S(1)} %copy-done.1, bf16[15,32,224]{2,1,0:T(8,128)(2,1)S(1)} %collective-permute-done, bf16[286,15,224]{2,1,0:T(8,128)(2,1)S(1)} %copy.11, ...), kind=kOutput, calls=%fused_computation.17 | convolution fusion | flops 293931584 | bytes 16144256 | tf_op jit(solution)/shard_map/lqb,qp->lpb/dot_general | solution.py:39
  105.8 0.0 copy-done.2
  105.8 18.1 %divide_subtract_fusion = f32[256,32,224]{0,2,1:T(8,128)S(1)} fusion(bf16[256,32,224]{0,2,1:T(8,128)(2,1)S(1)} %copy-done.2, f32[256,32]{0,1:T(8,128)S(1)} %broadcast_multiply_fusion.1, f32[286,32,224]{2,1,0:T(8,128)} %fusion.14, s32[256]{0:T(256)S(1)} %iota_add_fusion), kind=kOutput, calls=%fused_computation.13 | convolution fusion | flops 6303472128 | bytes 19244032 | tf_op jit(solution)/shard_map/kpb,kl->lpb/dot_general | solution.py:46
  123.9 3.0 copy-done
  126.9 1.8 fusion.20
  128.8 0.0 all-reduce.5.cloned.1.call-update
  128.8 9.9 %copy.14 = f32[256,32,224]{2,1,0:T(8,128)} copy(f32[256,32,224]{0,2,1:T(8,128)} %copy-done) | data formatting | bytes 14680064 | tf_op jit(solution)/shard_map/sub | solution.py:64
  138.7 113.2 %all-reduce.5.cloned.1.call-done = f32[224,224]{1,0:T(8,128)} async-done(((f32[224,224]{1,0:T(8,128)}), f32[224,224]{1,0:T(8,128)}) %all-reduce.5.cloned.1.call-update) | async-done | bytes 200720 | tf_op jit(solution)/shard_map/psum | solution.py:68
  251.9 1.6 select_reduce_fusion
  254.1 1.0 select_add_fusion
  255.1 0.1 copy.15
  255.2 1.0 fusion.29
  256.2 11.7 %cholesky.50 = f32[128,128]{1,0:T(8,128)S(1)} custom-call(f32[128,128]{1,0:T(8,128)S(1)} %cholesky.121), custom_call_target="Cholesky" | custom-call | tf_op jit(solution)/shard_map/jit(cholesky)/cholesky | solution.py:71
  268.0 9.8 %custom-call.15 = f32[1,128,128]{1,2,0:T(8,128)S(1)} custom-call(f32[1,128,128]{2,1,0:T(8,128)S(1)} %get-tuple-element.30), custom_call_target="InvertDiagBlocksLowerTriangular" | custom-call | tf_op jit(solution)/shard_map/jit(cholesky)/cholesky | solution.py:71
  277.8 0.2 constant_dynamic-update-slice_fusion.1
  278.0 0.2 convolution_subtract_fusion.1
  278.2 8.8 %cholesky.108 = f32[96,96]{1,0:T(8,128)S(1)} custom-call(f32[96,96]{1,0:T(8,128)S(1)} %convolution_subtract_fusion.1), custom_call_target="Cholesky" | custom-call | tf_op jit(solution)/shard_map/jit(cholesky)/cholesky | solution.py:71
  287.0 0.6 compare_reduce_fusion
  287.6 0.6 compare_reduce_fusion.1
  289.5 0.1 fusion.33
  289.7 19.7 %custom-call.16 = f32[2,128,128]{1,2,0:T(8,128)S(1)} custom-call(f32[2,128,128]{2,1,0:T(8,128)S(1)} %pad_maximum_fusion.1), custom_call_target="InvertDiagBlocksLowerTriangular" | custom-call | tf_op jit(solution)/shard_map/jit(_solve_triangular)/triangular_solve | solution.py:72
  309.3 0.3 fusion.31
  309.6 0.4 convolution_subtract_fusion
  310.0 0.4 fusion.37
  310.4 11.4 %fusion.19 = f32[8192]{0:T(1024)S(1)} fusion(f32[8192,224]{1,0:T(8,128)} %bitcast.37, f32[96,224]{0,1:T(8,128)S(1)} %fusion.37, f32[128,224]{0,1:T(8,128)S(1)} %fusion.31), kind=kOutput, calls=%fused_computation.18 | convolution fusion | flops 4936213504 | bytes 7573504 | tf_op jit(solution)/shard_map/dot_general | solution.py:73
  321.7 0.1 div.39
  321.8 0.7 copy.17
  (16 shorter events, 0.2 us)
Async XLA Ops:
  6.5 245.3 %all-reduce.5.cloned.1.call-start = ((), (), s32[]{:S(2)}) async-start(), calls=%async_computation | async-start | bytes 458752 | tf_op jit(solution)/shard_map/psum | solution.py:68
  15.5 8.6 %collective-permute-start = (bf16[15,32,224]{2,1,0:T(8,128)(2,1)S(1)}, bf16[15,32,224]{2,1,0:T(8,128)(2,1)S(1)}, u32[]{:S(2)}, u32[]{:S(2)}) collective-permute-start(bf16[15,32,224]{2,1,0:T(8,128)(2,1)S(1)} %get-tuple-element.27), channel_id=1, source_target_pairs={{0,8},{8,16},{16,24},{1,9},{9,17},{17,25},{2,10},{10,18},{18,26},{... | collective-permute-start | bytes 645128 | tf_op jit(solution)/shard_map/ppermute | solution.py:15
  19.5 8.4 %collective-permute-start.1 = (bf16[15,32,224]{2,1,0:T(8,128)(2,1)S(1)}, bf16[15,32,224]{2,1,0:T(8,128)(2,1)S(1)}, u32[]{:S(2)}, u32[]{:S(2)}) collective-permute-start(bf16[15,32,224]{2,1,0:T(8,128)(2,1)S(1)} %get-tuple-element.28), channel_id=1, source_target_pairs={{8,0},{16,8},{24,16},{9,1},{17,9},{25,17},{10,2},{18,10},{26,18},{... | collective-permute-start | bytes 645128 | tf_op jit(solution)/shard_map/ppermute | solution.py:18
  32.5 29.1 %collective-permute-start.2 = (bf16[286,15,224]{2,0,1:T(8,128)(2,1)S(1)}, bf16[286,15,224]{2,0,1:T(8,128)(2,1)}, u32[]{:S(2)}, u32[]{:S(2)}) collective-permute-start(bf16[286,15,224]{2,0,1:T(8,128)(2,1)S(1)} %copy.9), channel_id=1, source_target_pairs={{0,1},{1,2},{2,3},{3,4},{4,5},{5,6},{6,7},{8,9},{9,10},{10,11},{11... | collective-permute-start | bytes 5765768 | tf_op jit(solution)/shard_map/ppermute | solution.py:15
  39.6 47.5 %collective-permute-start.3 = (bf16[286,15,224]{2,0,1:T(8,128)(2,1)}, bf16[286,15,224]{2,0,1:T(8,128)(2,1)}, u32[]{:S(2)}, u32[]{:S(2)}) collective-permute-start(bf16[286,15,224]{2,0,1:T(8,128)(2,1)} %copy.10), channel_id=1, source_target_pairs={{1,0},{2,1},{3,2},{4,3},{5,4},{6,5},{7,6},{9,8},{10,9},{11,10},{12... | collective-permute-start | bytes 5765768 | tf_op jit(solution)/shard_map/ppermute | solution.py:18
  41.5 48.4 %copy-start.1 = (bf16[256,32,224]{2,1,0:T(8,128)(2,1)S(1)}, bf16[256,32,224]{2,1,0:T(8,128)(2,1)}, u32[]{:S(2)}) copy-start(bf16[256,32,224]{2,1,0:T(8,128)(2,1)} %copy.6) | copy-start | bytes 11010052
  89.9 15.9 %copy-start.2 = (bf16[256,32,224]{0,2,1:T(8,128)(2,1)S(1)}, bf16[256,32,224]{0,2,1:T(8,128)(2,1)}, u32[]{:S(2)}) copy-start(bf16[256,32,224]{0,2,1:T(8,128)(2,1)} %param.1) | copy-start | bytes 11010052
  123.9 3.0 copy-start
Sparse Core Ops, SparseCore 0:
  128.9 122.8 all-reduce.4
where the time goes:
time: 330 us; the launch traced here: 329 us
  waiting for transfers between devices  163 us (49%)
  other arithmetic  57.8 us (18%)
  matrix products  48.6 us (15%)
  local copies, waits for them, and re-layouts  32.5 us (10%)
  between operations  15.6 us (5%)
  starting transfers between devices  12.1 us (4%)
    psum x1, waiting for transfers between devices, shards(): lax.psum(partial_cov, ('track', 'cross')) / (total_lines * total_pix)  113 us
    another operation x7, other arithmetic, shards(): factor = jnp.linalg.cholesky(loaded)  31.6 us
    ppermute x2, waiting for transfers between devices, with_halo(): lax.ppermute(lax.slice_in_dim(block, 0, width, axis=dim), axis, backward)  26.4 us
    ppermute x2, waiting for transfers between devices, with_halo(): lax.ppermute(lax.slice_in_dim(block, block.shape[dim] - width, None, axis...  23.2 us
    another operation x6, other arithmetic, shards(): inverse = jax.scipy.linalg.solve_triangular(factor, identity, lower=True)  19.8 us
    dot_general x1, matrix products, sum_lines(): jnp.einsum('kpb,kl->lpb', values, weights, precision=precision, preferred...  18.1 us
    dot_general x1, matrix products, sum_pixels(): jnp.einsum('lqb,qp->lpb', values, weights, precision=None, preferred_elem...  15.9 us
    dot_general x1, matrix products, shards(): jnp.dot(flat, inverse.T, precision=highest, preferred_element_type=jnp.fl...  11.4 us
  transfers between devices with their start and end apart: 5, of which 5 were waited for; matrix products, arithmetic and copies ran while one was open for 5% of the time, Pallas kernels for 0%

commit v1 on v0

--- a/solution.py
+++ b/solution.py
@@ -65,7 +65,9 @@
     flat = residual.reshape(lines_dev * pix_dev, bands)
     flat_bf = flat.astype(jnp.bfloat16)
     partial_cov = jnp.dot(flat_bf.T, flat_bf, preferred_element_type=jnp.float32)
-    covariance = lax.psum(partial_cov, ("track", "cross")) / (total_lines * total_pix)
+    covariance = jnp.sum(lax.all_gather(partial_cov, ("track", "cross")), axis=0) / (
+        total_lines * total_pix
+    )
     identity = jnp.eye(bands, dtype=jnp.float32)
     loaded = covariance + LOAD * (jnp.trace(covariance) / bands) * identity
     factor = jnp.linalg.cholesky(loaded)

time: 330 us -> 281 us (0.85)
  waiting for transfers between devices: 163 us -> 113 us
    psum x1 -> x0, waiting for transfers between devices: 113 us -> none  [shards(): lax.psum(partial_cov, ('track', 'cross')) / (total_lines * total_pix)]
    all_gather x0 -> x1, waiting for transfers between devices: none -> 62.9 us  [shards(): lax.all_gather(partial_cov, ('track', 'cross'))]
    reduce_sum x0 -> x1, other arithmetic: none -> 3.61 us  [shards(): jnp.sum(lax.all_gather(partial_cov, ('track', 'cross')), axis=0)]
where the time goes in v1:
time: 281 us; the launch traced here: 280 us
  waiting for transfers between devices  113 us (40%)
  other arithmetic  58.9 us (21%)
  matrix products  48.3 us (17%)
  local copies, waits for them, and re-layouts  32.5 us (12%)
  between operations  15.6 us (6%)
  starting transfers between devices  12.1 us (4%)
    all_gather x1, waiting for transfers between devices, shards(): lax.all_gather(partial_cov, ('track', 'cross'))  62.9 us
    another operation x7, other arithmetic, shards(): factor = jnp.linalg.cholesky(loaded)  31.6 us
    ppermute x2, waiting for transfers between devices, with_halo(): lax.ppermute(lax.slice_in_dim(block, 0, width, axis=dim), axis, backward)  26.4 us
    ppermute x2, waiting for transfers between devices, with_halo(): lax.ppermute(lax.slice_in_dim(block, block.shape[dim] - width, None, axis...  23.3 us
    another operation x6, other arithmetic, shards(): inverse = jax.scipy.linalg.solve_triangular(factor, identity, lower=True)  20.1 us
    dot_general x1, matrix products, sum_lines(): jnp.einsum('kpb,kl->lpb', values, weights, precision=precision, preferred...  18.1 us
    dot_general x1, matrix products, sum_pixels(): jnp.einsum('lqb,qp->lpb', values, weights, precision=None, preferred_elem...  15.9 us
    dot_general x1, matrix products, shards(): jnp.dot(flat, inverse.T, precision=highest, preferred_element_type=jnp.fl...  11.1 us
  transfers between devices with their start and end apart: 5, of which 5 were waited for; matrix products, arithmetic and copies ran while one was open for 5% of the time, Pallas kernels for 0%

profile of v1, /device:TPU:1, one launch (start us, length us, event | category | flops | bytes accessed | tf_op | source)
XLA Modules:
  0.0 279.9 jit_solution(10358949035751982908)
XLA Ops:
  6.5 0.0 all-gather.3.cloned.1.call-start
  6.5 7.8 %copy.6 = bf16[256,32,224]{2,1,0:T(8,128)(2,1)} copy(bf16[256,32,224]{0,2,1:T(8,128)(2,1)} %param.1) | data formatting | bytes 7340032 | tf_op args[0]
  14.4 1.1 fusion.45
  15.5 4.0 %collective-permute-start = (bf16[15,32,224]{2,1,0:T(8,128)(2,1)S(1)}, bf16[15,32,224]{2,1,0:T(8,128)(2,1)S(1)}, u32[]{:S(2)}, u32[]{:S(2)}) collective-permute-start(bf16[15,32,224]{2,1,0:T(8,128)(2,1)S(1)} %get-tuple-element.27), channel_id=1, source_target_pairs={{0,8},{8,16},{16,24},{1,9},{9,17},{17,25},{2,10},{10,18},{18,26},{... | collective-permute-start | bytes 645128 | tf_op jit(solution)/shard_map/ppermute | solution.py:15
  19.5 1.3 collective-permute-start.1
  20.8 3.3 %collective-permute-done = bf16[15,32,224]{2,1,0:T(8,128)(2,1)S(1)} collective-permute-done((bf16[15,32,224]{2,1,0:T(8,128)(2,1)S(1)}, bf16[15,32,224]{2,1,0:T(8,128)(2,1)S(1)}, u32[]{:S(2)}, u32[]{:S(2)}) %collective-permute-start) | collective-permute-done | bytes 215072 | tf_op jit(solution)/shard_map/ppermute | solution.py:15
  24.1 3.8 %collective-permute-done.1 = bf16[15,32,224]{2,1,0:T(8,128)(2,1)S(1)} collective-permute-done((bf16[15,32,224]{2,1,0:T(8,128)(2,1)S(1)}, bf16[15,32,224]{2,1,0:T(8,128)(2,1)S(1)}, u32[]{:S(2)}, u32[]{:S(2)}) %collective-permute-start.1) | collective-permute-done | bytes 215072 | tf_op jit(solution)/shard_map/ppermute | solution.py:18
  27.9 2.7 pad_maximum_fusion
  30.7 1.0 fusion.44
  31.7 0.8 copy.9
  32.5 4.9 %collective-permute-start.2 = (bf16[286,15,224]{2,0,1:T(8,128)(2,1)S(1)}, bf16[286,15,224]{2,0,1:T(8,128)(2,1)}, u32[]{:S(2)}, u32[]{:S(2)}) collective-permute-start(bf16[286,15,224]{2,0,1:T(8,128)(2,1)S(1)} %copy.9), channel_id=1, source_target_pairs={{0,1},{1,2},{2,3},{3,4},{4,5},{5,6},{6,7},{8,9},{9,10},{10,11},{11... | collective-permute-start | bytes 5765768 | tf_op jit(solution)/shard_map/ppermute | solution.py:15
  37.4 2.1 copy.10
  39.6 1.9 collective-permute-start.3
  41.5 0.0 copy-start.1
  41.5 0.1 broadcast_multiply_fusion.1
  41.6 20.0 %collective-permute-done.2 = bf16[286,15,224]{2,0,1:T(8,128)(2,1)} collective-permute-done((bf16[286,15,224]{2,0,1:T(8,128)(2,1)S(1)}, bf16[286,15,224]{2,0,1:T(8,128)(2,1)}, u32[]{:S(2)}, u32[]{:S(2)}) %collective-permute-start.2) | collective-permute-done | bytes 1921952 | tf_op jit(solution)/shard_map/ppermute | solution.py:15
  61.6 2.9 %copy.11 = bf16[286,15,224]{2,1,0:T(8,128)(2,1)S(1)} copy(bf16[286,15,224]{2,0,1:T(8,128)(2,1)} %collective-permute-done.2) | data formatting | bytes 3843840 | tf_op jit(solution)/shard_map/ppermute | solution.py:15
  64.5 22.6 %collective-permute-done.3 = bf16[286,15,224]{2,0,1:T(8,128)(2,1)} collective-permute-done((bf16[286,15,224]{2,0,1:T(8,128)(2,1)}, bf16[286,15,224]{2,0,1:T(8,128)(2,1)}, u32[]{:S(2)}, u32[]{:S(2)}) %collective-permute-start.3) | collective-permute-done | bytes 1921952 | tf_op jit(solution)/shard_map/ppermute | solution.py:18
  87.1 2.9 %copy.12 = bf16[286,15,224]{2,1,0:T(8,128)(2,1)S(1)} copy(bf16[286,15,224]{2,0,1:T(8,128)(2,1)} %collective-permute-done.3) | data formatting | bytes 3843840 | tf_op jit(solution)/shard_map/ppermute | solution.py:18
  89.9 0.0 copy-done.1
  89.9 0.0 copy-start.2
  89.9 15.9 %fusion.14 = f32[286,32,224]{2,1,0:T(8,128)} fusion(bf16[286,15,224]{2,1,0:T(8,128)(2,1)S(1)} %copy.12, bf16[15,32,224]{2,1,0:T(8,128)(2,1)S(1)} %collective-permute-done.1, bf16[256,32,224]{2,1,0:T(8,128)(2,1)S(1)} %copy-done.1, bf16[15,32,224]{2,1,0:T(8,128)(2,1)S(1)} %collective-permute-done, bf16[286,15,224]{2,1,0:T(8,128)(2,1)S(1)} %copy.11, ...), kind=kOutput, calls=%fused_computation.17 | convolution fusion | flops 293931584 | bytes 16144256 | tf_op jit(solution)/shard_map/lqb,qp->lpb/dot_general | solution.py:39
  105.8 0.0 copy-done.2
  105.8 18.1 %divide_subtract_fusion = f32[256,32,224]{0,2,1:T(8,128)S(1)} fusion(bf16[256,32,224]{0,2,1:T(8,128)(2,1)S(1)} %copy-done.2, f32[256,32]{0,1:T(8,128)S(1)} %broadcast_multiply_fusion.1, f32[286,32,224]{2,1,0:T(8,128)} %fusion.14, s32[256]{0:T(256)S(1)} %iota_add_fusion), kind=kOutput, calls=%fused_computation.13 | convolution fusion | flops 6303472128 | bytes 19244032 | tf_op jit(solution)/shard_map/kpb,kl->lpb/dot_general | solution.py:46
  123.9 3.0 %copy-done = f32[256,32,224]{0,2,1:T(8,128)} copy-done((f32[256,32,224]{0,2,1:T(8,128)}, f32[256,32,224]{0,2,1:T(8,128)S(1)}, u32[]{:S(2)}) %copy-start) | copy-done | bytes 7340056
  126.9 1.8 fusion.20
  128.7 0.0 all-gather.3.cloned.1.call-update
  128.8 9.9 %copy.14 = f32[256,32,224]{2,1,0:T(8,128)} copy(f32[256,32,224]{0,2,1:T(8,128)} %copy-done) | data formatting | bytes 14680064 | tf_op jit(solution)/shard_map/sub | solution.py:64
  138.7 62.9 %all-gather.3.cloned.1.call-done = f32[7168,224]{1,0:T(8,128)} async-done(((f32[224,224]{1,0:T(8,128)}), f32[7168,224]{1,0:T(8,128)}) %all-gather.3.cloned.1.call-update) | async-done | bytes 6422544 | tf_op jit(solution)/shard_map/all_gather | solution.py:68
  201.6 3.6 %reduce_sum.28 = f32[224,224]{1,0:T(8,128)S(1)} reduce(f32[32,224,224]{2,1,0:T(8,128)} %bitcast.37, f32[]{:T(128)} %constant.127.clone.1), dimensions={0}, to_apply=%region_0.0 | reduce | flops 1555456 | bytes 6623236 | tf_op jit(solution)/shard_map/reduce_sum | solution.py:68
  205.2 0.6 select_reduce_fusion
  205.8 0.1 copy.15
  206.6 0.1 add_multiply_fusion
  206.7 11.7 %cholesky.50 = f32[128,128]{1,0:T(8,128)S(1)} custom-call(f32[128,128]{1,0:T(8,128)S(1)} %cholesky.121), custom_call_target="Cholesky" | custom-call | tf_op jit(solution)/shard_map/jit(cholesky)/cholesky | solution.py:73
  218.5 9.8 %custom-call.15 = f32[1,128,128]{1,2,0:T(8,128)S(1)} custom-call(f32[1,128,128]{2,1,0:T(8,128)S(1)} %get-tuple-element.32), custom_call_target="InvertDiagBlocksLowerTriangular" | custom-call | tf_op jit(solution)/shard_map/jit(cholesky)/cholesky | solution.py:73
  228.3 0.2 constant_dynamic-update-slice_fusion.1
  228.5 0.2 convolution_subtract_fusion.1
  228.7 8.8 %cholesky.108 = f32[96,96]{1,0:T(8,128)S(1)} custom-call(f32[96,96]{1,0:T(8,128)S(1)} %convolution_subtract_fusion.1), custom_call_target="Cholesky" | custom-call | tf_op jit(solution)/shard_map/jit(cholesky)/cholesky | solution.py:73
  237.5 0.6 compare_reduce_fusion
  238.1 0.6 compare_reduce_fusion.1
  240.0 0.1 fusion.32
  240.1 19.9 %custom-call.16 = f32[2,128,128]{1,2,0:T(8,128)S(1)} custom-call(f32[2,128,128]{2,1,0:T(8,128)S(1)} %pad_maximum_fusion.1), custom_call_target="InvertDiagBlocksLowerTriangular" | custom-call | tf_op jit(solution)/shard_map/jit(_solve_triangular)/triangular_solve | solution.py:74
  260.1 0.3 fusion.30
  260.4 0.4 convolution_subtract_fusion
  260.7 0.4 fusion.36
  261.1 11.1 %fusion.19 = f32[8192]{0:T(1024)S(1)} fusion(f32[8192,224]{1,0:T(8,128)} %bitcast.36, f32[96,224]{0,1:T(8,128)S(1)} %fusion.36, f32[128,224]{0,1:T(8,128)S(1)} %fusion.30), kind=kOutput, calls=%fused_computation.18 | convolution fusion | flops 4936213504 | bytes 7573504 | tf_op jit(solution)/shard_map/dot_general | solution.py:75
  272.2 0.1 div.42
  272.3 0.7 copy.17
  (16 shorter events, 0.2 us)
Async XLA Ops:
  6.5 195.1 %all-gather.3.cloned.1.call-start = ((), (), s32[]{:S(2)}) async-start(), calls=%async_computation | async-start | bytes 7569408 | tf_op jit(solution)/shard_map/all_gather | solution.py:68
  15.5 8.6 %collective-permute-start = (bf16[15,32,224]{2,1,0:T(8,128)(2,1)S(1)}, bf16[15,32,224]{2,1,0:T(8,128)(2,1)S(1)}, u32[]{:S(2)}, u32[]{:S(2)}) collective-permute-start(bf16[15,32,224]{2,1,0:T(8,128)(2,1)S(1)} %get-tuple-element.27), channel_id=1, source_target_pairs={{0,8},{8,16},{16,24},{1,9},{9,17},{17,25},{2,10},{10,18},{18,26},{... | collective-permute-start | bytes 645128 | tf_op jit(solution)/shard_map/ppermute | solution.py:15
  19.5 8.4 %collective-permute-start.1 = (bf16[15,32,224]{2,1,0:T(8,128)(2,1)S(1)}, bf16[15,32,224]{2,1,0:T(8,128)(2,1)S(1)}, u32[]{:S(2)}, u32[]{:S(2)}) collective-permute-start(bf16[15,32,224]{2,1,0:T(8,128)(2,1)S(1)} %get-tuple-element.28), channel_id=1, source_target_pairs={{8,0},{16,8},{24,16},{9,1},{17,9},{25,17},{10,2},{18,10},{26,18},{... | collective-permute-start | bytes 645128 | tf_op jit(solution)/shard_map/ppermute | solution.py:18
  32.5 29.1 %collective-permute-start.2 = (bf16[286,15,224]{2,0,1:T(8,128)(2,1)S(1)}, bf16[286,15,224]{2,0,1:T(8,128)(2,1)}, u32[]{:S(2)}, u32[]{:S(2)}) collective-permute-start(bf16[286,15,224]{2,0,1:T(8,128)(2,1)S(1)} %copy.9), channel_id=1, source_target_pairs={{0,1},{1,2},{2,3},{3,4},{4,5},{5,6},{6,7},{8,9},{9,10},{10,11},{11... | collective-permute-start | bytes 5765768 | tf_op jit(solution)/shard_map/ppermute | solution.py:15
  39.6 47.5 %collective-permute-start.3 = (bf16[286,15,224]{2,0,1:T(8,128)(2,1)}, bf16[286,15,224]{2,0,1:T(8,128)(2,1)}, u32[]{:S(2)}, u32[]{:S(2)}) collective-permute-start(bf16[286,15,224]{2,0,1:T(8,128)(2,1)} %copy.10), channel_id=1, source_target_pairs={{1,0},{2,1},{3,2},{4,3},{5,4},{6,5},{7,6},{9,8},{10,9},{11,10},{12... | collective-permute-start | bytes 5765768 | tf_op jit(solution)/shard_map/ppermute | solution.py:18
  41.5 48.4 %copy-start.1 = (bf16[256,32,224]{2,1,0:T(8,128)(2,1)S(1)}, bf16[256,32,224]{2,1,0:T(8,128)(2,1)}, u32[]{:S(2)}) copy-start(bf16[256,32,224]{2,1,0:T(8,128)(2,1)} %copy.6) | copy-start | bytes 11010052
  89.9 15.9 %copy-start.2 = (bf16[256,32,224]{0,2,1:T(8,128)(2,1)S(1)}, bf16[256,32,224]{0,2,1:T(8,128)(2,1)}, u32[]{:S(2)}) copy-start(bf16[256,32,224]{0,2,1:T(8,128)(2,1)} %param.1) | copy-start | bytes 11010052
  123.9 3.0 %copy-start = (f32[256,32,224]{0,2,1:T(8,128)}, f32[256,32,224]{0,2,1:T(8,128)S(1)}, u32[]{:S(2)}) copy-start(f32[256,32,224]{0,2,1:T(8,128)S(1)} %divide_subtract_fusion) | copy-start | bytes 22020100
Sparse Core Ops, SparseCore 0:
  128.9 72.6 all-gather.2
